TPU v7x, 256 devices: a whole 4x4x8 slice. The times are simulated.
256 devices in a mesh: space: 4 (over z_lo), rows: 8 (over y, core), cols: 8 (over z_hi, x).
Axes of the slice: x: 4, y: 4, z: 8 (z_hi: 2, z_lo: 4; z = z_hi * 4 + z_lo), core: 2. Of those that a mesh axis runs over, the one named last changes fastest.
Arguments:
- occupation: float32 [12288, 2048], P(('cols', 'rows'), 'space'), may hold values from -13.5 to 13.5, as said below
- propagator: float32 [12288, 12288], P('rows', 'cols'), may hold values from -0.5 to 1, as said below
- flags_first: int32 [12288, 2048], P(('cols', 'rows'), 'space'), may hold values from 0 to 2
- flags_second: int32 [12288, 2048], P(('rows', 'cols'), 'space'), may hold values from 0 to 2
- courant: float32 [12288], replicated, may hold values from -0.9 to 0.9
- weights: float32 [12288], replicated, may hold values from 0.5 to 6
Outputs:
- occupation_out: float32 [12288, 2048], P(('cols', 'rows'), 'space')
- temperature: float32 [2048], P('space')
Inputs may be any that keep to these rules, and one draw needn't show every extreme that they name: occupation varies from mode to mode and cell to cell. propagator equals its transpose.
All inputs are finite; a program needn't handle non-finite values.
Results may differ from a plain program's by a relative error of at most 0.0003.
Values sent between devices are 32-bit elements; how exact they have to be, the bound alone decides.
No kernel may reach another device: no remote copies, remote signals or barrier semaphores. Data moves between devices by JAX's collectives and lax.ppermute only.
A program may use at most 64 MiB of HBM per device.

v0:
```python
import jax
import jax.numpy as jnp
from jax import lax
from jax.sharding import PartitionSpec as P

highest = lax.Precision.HIGHEST


def padded_2(block, sides, width):
    for axis, dim in sides:
        count = lax.axis_size(axis)
        forward = [(i, i + 1) for i in range(count - 1)]
        backward = [(target, source) for source, target in forward]
        low = lax.ppermute(
            lax.slice_in_dim(block, block.shape[dim] - width, None, axis=dim), axis, forward
        )
        high = lax.ppermute(lax.slice_in_dim(block, 0, width, axis=dim), axis, backward)
        block = jnp.concatenate([low, block, high], axis=dim)
    return block


def limited(left_diff, right_diff, selector):
    left_size = jnp.abs(left_diff)
    right_size = jnp.abs(right_diff)
    agreement = 0.5 * (jnp.sign(left_diff) + jnp.sign(right_diff))
    minmod_size = jnp.minimum(left_size, right_size)
    central_size = jnp.minimum(2.0 * minmod_size, 0.5 * jnp.abs(left_diff + right_diff))
    superbee_size = jnp.maximum(
        jnp.minimum(2.0 * left_size, right_size), jnp.minimum(left_size, 2.0 * right_size)
    )
    chosen = jnp.where(
        selector == 0.0, minmod_size, jnp.where(selector == 1.0, central_size, superbee_size)
    )
    return agreement * chosen


def advect(padded, selector, courant_col):
    differences = padded[:, 1:] - padded[:, :-1]
    slopes = limited(differences[:, :-1], differences[:, 1:], selector[:, 1:-1])
    centers = padded[:, 1:-1]
    forward = courant_col * (centers[:, :-1] + 0.5 * (1.0 - courant_col) * slopes[:, :-1])
    backward = courant_col * (centers[:, 1:] - 0.5 * (1.0 + courant_col) * slopes[:, 1:])
    fluxes = jnp.where(courant_col > 0.0, forward, backward)
    return padded[:, 2:-2] - (fluxes[:, 1:] - fluxes[:, :-1])


def advect_slab(field, selector, courant_part):
    stacked = jnp.stack([field, selector.astype(jnp.float32)])
    padded = padded_2(stacked, (("space", 2),), 2)
    return advect(padded[0], padded[1], courant_part[:, None])


def heat_all(weight_part, shifted):
    return lax.psum(jnp.dot(weight_part, shifted, precision=highest), ("rows", "cols"))


def on_device(occupation, propagator, flags_first, flags_second, courant, weights):
    row_count = lax.axis_size("rows")
    col_count = lax.axis_size("cols")
    row_index = lax.axis_index("rows")
    col_index = lax.axis_index("cols")
    local_modes = occupation.shape[0]
    weight_total = jnp.sum(weights)
    offset_first = (col_index * row_count + row_index) * local_modes
    weight_first = lax.dynamic_slice_in_dim(weights, offset_first, local_modes)
    courant_first = lax.dynamic_slice_in_dim(courant, offset_first, local_modes)
    shifted = advect_slab(occupation, flags_first, courant_first)
    heat = heat_all(weight_first, shifted) / weight_total
    deviation = shifted - weight_first[:, None] * heat[None, :]
    partial_value = jnp.dot(
        propagator,
        lax.all_gather(deviation, "rows", axis=0, tiled=True),
        precision=highest,
        preferred_element_type=jnp.float32,
    )
    summed = lax.psum_scatter(partial_value, "cols", scatter_dimension=0, tiled=True)
    offset_second = (row_index * col_count + col_index) * local_modes
    weight_second = lax.dynamic_slice_in_dim(weights, offset_second, local_modes)
    courant_second = lax.dynamic_slice_in_dim(courant, offset_second, local_modes)
    middle = summed + weight_second[:, None] * heat[None, :]
    shifted_second = advect_slab(middle, flags_second, courant_second)
    heat_second = heat_all(weight_second, shifted_second) / weight_total
    deviation_second = shifted_second - weight_second[:, None] * heat_second[None, :]
    partial_second = lax.dot_general(
        propagator,
        lax.all_gather(deviation_second, "cols", axis=0, tiled=True),
        (((0,), (0,)), ((), ())),
        precision=highest,
        preferred_element_type=jnp.float32,
    )
    final = lax.psum_scatter(partial_second, "rows", scatter_dimension=0, tiled=True)
    final = final + weight_first[:, None] * heat_second[None, :]
    return (final, heat_second)


def solution(mesh):
    placed = (
        P(("cols", "rows"), "space"),
        P("rows", "cols"),
        P(("cols", "rows"), "space"),
        P(("rows", "cols"), "space"),
        P(),
        P(),
    )
    return jax.shard_map(
        on_device,
        mesh=mesh,
        in_specs=placed,
        out_specs=(P(("cols", "rows"), "space"), P("space")),
        check_vma=False,
    )
```

profile of v0, /device:TPU:2, one launch (start us, length us, event | category | flops | bytes accessed | tf_op | source)
XLA Modules:
  0.0 767.8 jit_solution(1499970193836055959)
XLA Ops:
  7.2 0.0 all-gather.3.cloned.1.call-start
  7.2 1.0 convert_bitcast_fusion.1
  8.2 1.1 pad_maximum_fusion.5
  9.3 3.8 collective-permute-start
  13.1 1.3 collective-permute-start.1
  14.4 0.9 broadcast_compare_fusion
  15.3 0.9 fusion.16
  16.2 1.4 reduce_sum.9
  17.6 0.0 collective-permute-done
  17.6 4.0 collective-permute-done.1
  21.6 1.4 pad_maximum_fusion
  22.9 0.1 slice_bitcast_fusion.2
  23.0 0.2 slice_subtract_fusion.1
  23.2 0.6 select_multiply_fusion.1
  23.8 0.6 fusion.7
  24.4 0.5 fusion.12
  24.9 201.8 %psum.14 = f32[512]{0:T(512)S(1)} all-reduce(f32[512]{0:T(512)S(1)} %bitcast.35), channel_id=1, replica_groups=mesh['space'=4,'rows'=8,'cols'=8] {'rows','cols'}, use_global_device_ids=true, to_apply=%region_0.0 | all-reduce | flops 512 | bytes 4096 | tf_op jit(solution)/shard_map/psum | solution.py:54
  226.7 0.6 broadcast_divide_fusion.1
  227.4 1.1 multiply_subtract_fusion.1
  228.4 0.0 all-gather.3.cloned.1.call-update
  228.5 0.0 reduce-scatter.7.cloned.1.call-start
  228.5 30.8 %all-gather.3.cloned.1.call-done = f32[1536,512]{1,0:T(8,128)} async-done(((f32[192,512]{1,0:T(8,128)}), f32[1536,512]{1,0:T(8,128)}) %all-gather.3.cloned.1.call-update) | async-done | bytes 3145744 | tf_op jit(solution)/shard_map/all_gather | solution.py:72
  259.3 33.2 %convolution_bitcast_fusion.1 = f32[1536,512]{0,1:T(8,128)S(1)} fusion(f32[1536,512]{1,0:T(8,128)} %all-gather.3.cloned.1.call-done, f32[1536,1536]{1,0:T(8,128)} %param.7), kind=kOutput, calls=%fused_computation.1 | convolution fusion | flops 14495514624 | bytes 15728640 | tf_op jit(solution)/shard_map/dot_general | solution.py:70
  292.4 2.3 copy.14
  294.8 0.0 copy-start
  294.8 0.0 reduce-scatter.7.cloned.1.call-update
  294.8 0.0 all-gather.5.cloned.1.call-start
  294.8 0.9 copy-done
  295.8 106.0 %reduce-scatter.7.cloned.1.call-done = f32[192,512]{1,0:T(8,128)} async-done(((f32[1536,512]{1,0:T(8,128)}), f32[192,512]{1,0:T(8,128)}) %reduce-scatter.7.cloned.1.call-update) | async-done | bytes 393232 | tf_op jit(solution)/shard_map/reduce_scatter | solution.py:76
  401.8 1.1 add_bitcast_fusion
  402.9 0.1 pad_maximum_fusion.3
  403.0 1.7 collective-permute-start.2
  404.7 1.3 collective-permute-start.3
  406.0 1.8 collective-permute-done.2
  407.9 4.4 collective-permute-done.3
  412.3 0.4 pad_maximum_fusion.1
  412.7 0.1 slice_bitcast_fusion
  412.7 0.2 slice_subtract_fusion
  412.9 0.6 select_multiply_fusion
  413.5 0.6 fusion.2
  414.1 0.5 fusion.14
  414.6 202.1 %psum.15 = f32[512]{0:T(512)S(1)} all-reduce(f32[512]{0:T(512)S(1)} %bitcast.36), channel_id=1, replica_groups=mesh['space'=4,'rows'=8,'cols'=8] {'rows','cols'}, use_global_device_ids=true, to_apply=%region_3.4 | all-reduce | flops 512 | bytes 4096 | tf_op jit(solution)/shard_map/psum | solution.py:54
  616.8 0.6 broadcast_divide_fusion
  617.4 0.0 copy-start.1
  617.4 1.0 multiply_subtract_fusion
  618.5 0.0 all-gather.5.cloned.1.call-update
  618.5 0.0 reduce-scatter.9.cloned.1.call-start
  618.6 84.9 %all-gather.5.cloned.1.call-done = f32[1536,512]{1,0:T(8,128)} async-done(((f32[192,512]{1,0:T(8,128)}), f32[1536,512]{1,0:T(8,128)}) %all-gather.5.cloned.1.call-update) | async-done | bytes 3145744 | tf_op jit(solution)/shard_map/all_gather | solution.py:86
  703.4 19.2 %convolution_bitcast_fusion = f32[1536,512]{0,1:T(8,128)S(1)} fusion(f32[1536,512]{1,0:T(8,128)} %all-gather.5.cloned.1.call-done, f32[1536,1536]{1,0:T(8,128)} %param.7), kind=kOutput, calls=%fused_computation | convolution fusion | flops 14495514624 | bytes 15728640 | tf_op jit(solution)/shard_map/dot_general | solution.py:84
  722.6 2.3 copy.16
  724.9 0.0 reduce-scatter.9.cloned.1.call-update
  725.0 34.5 %reduce-scatter.9.cloned.1.call-done = f32[192,512]{1,0:T(8,128)} async-done(((f32[1536,512]{1,0:T(8,128)}), f32[192,512]{1,0:T(8,128)}) %reduce-scatter.9.cloned.1.call-update) | async-done | bytes 393232 | tf_op jit(solution)/shard_map/reduce_scatter | solution.py:91
  759.4 0.0 copy-done.1
  759.4 1.8 multiply_add_fusion
  (3 shorter events, 0.0 us)
Async XLA Ops:
  7.2 252.1 %all-gather.3.cloned.1.call-start = ((), (), s32[]{:S(2)}) async-start(), calls=%async_computation.2 | async-start | bytes 3538944 | tf_op jit(solution)/shard_map/all_gather | solution.py:72
  9.3 8.3 %collective-permute-start = (f32[2,192,2]{2,1,0:T(8,128)S(1)}, f32[2,192,2]{2,1,0:T(8,128)S(1)}, u32[]{:S(2)}, u32[]{:S(2)}) collective-permute-start(f32[2,192,2]{2,1,0:T(8,128)S(1)} %get-tuple-element.14), channel_id=1, source_target_pairs={{0,64},{64,128},{128,192},{1,65},{65,129},{129,193},{2,66},{66,130... | collective-permute-start | bytes 9224 | tf_op jit(solution)/shard_map/ppermute | solution.py:14
  13.1 8.4 %collective-permute-start.1 = (f32[2,192,2]{2,1,0:T(8,128)S(1)}, f32[2,192,2]{2,1,0:T(8,128)S(1)}, u32[]{:S(2)}, u32[]{:S(2)}) collective-permute-start(f32[2,192,2]{2,1,0:T(8,128)S(1)} %get-tuple-element.15), channel_id=1, source_target_pairs={{64,0},{128,64},{192,128},{65,1},{129,65},{193,129},{66,2},{130,66... | collective-permute-start | bytes 9224 | tf_op jit(solution)/shard_map/ppermute | solution.py:17
  228.5 173.3 %reduce-scatter.7.cloned.1.call-start = ((), (), s32[]{:S(2)}) async-start(), calls=%async_computation.4 | async-start | bytes 3538944 | tf_op jit(solution)/shard_map/reduce_scatter | solution.py:76
  294.8 1.0 copy-start
  294.8 408.6 %all-gather.5.cloned.1.call-start = ((), (), s32[]{:S(2)}) async-start(), calls=%async_computation.3 | async-start | bytes 3538944 | tf_op jit(solution)/shard_map/all_gather | solution.py:86
  403.0 4.9 collective-permute-start.2
  404.7 7.6 collective-permute-start.3
  617.4 142.0 %copy-start.1 = (f32[512]{0:T(512)}, f32[512]{0:T(512)S(1)}, u32[]{:S(2)}) copy-start(f32[512]{0:T(512)S(1)} %broadcast_divide_fusion) | copy-start | bytes 6148
  618.5 140.9 %reduce-scatter.9.cloned.1.call-start = ((), (), s32[]{:S(2)}) async-start(), calls=%async_computation.5 | async-start | bytes 3538944 | tf_op jit(solution)/shard_map/reduce_scatter | solution.py:91
Sparse Core Ops, SparseCore 0:
  228.6 30.6 all-gather.2
  294.9 106.8 reduce-scatter.6
  618.6 84.7 all-gather.4
  725.1 34.3 reduce-scatter.8
where the time goes:
time: 768 us
  blocking collectives  404 us (53%)
  waiting for transfers between devices  266 us (35%)
  matrix products  53.3 us (7%)
  other arithmetic  15.3 us (2%)
  between operations  14 us (2%)
  starting transfers between devices  8.28 us (1%)
    psum x2, blocking collectives, heat_all(): lax.psum(jnp.dot(weight_part, shifted, precision=highest), ('rows', 'cols'))  404 us
    reduce_scatter x1, waiting for transfers between devices, on_device(): lax.psum_scatter(partial_value, 'cols', scatter_dimension=0, tiled=True)  106 us
    all_gather x1, waiting for transfers between devices, on_device(): lax.all_gather(deviation_second, 'cols', axis=0, tiled=True)  84.9 us
    reduce_scatter x1, waiting for transfers between devices, on_device(): lax.psum_scatter(partial_second, 'rows', scatter_dimension=0, tiled=True)  34.5 us
    dot_general x1, matrix products, on_device(): jnp.dot(propagator, lax.all_gather(deviation, 'rows', axis=0, tiled=True)...  33.2 us
    all_gather x1, waiting for transfers between devices, on_device(): lax.all_gather(deviation, 'rows', axis=0, tiled=True)  30.8 us
    dot_general x1, matrix products, on_device(): lax.dot_general(propagator, lax.all_gather(deviation_second, 'cols', axis...  19.2 us
  transfers between devices with their start and end apart: 8, of which 7 were waited for; matrix products, arithmetic and copies ran while one was open for 0% of the time, Pallas kernels for 0%

commit v1 on v0

v1 whole, which is shorter than its diff:
```python
import jax
import jax.numpy as jnp
from jax import lax
from jax.sharding import Mesh
from jax.sharding import PartitionSpec as P

highest = lax.Precision.HIGHEST
high = lax.Precision.HIGH

ROWS = ("y", "core")
COLS = ("zh", "x")


def padded_2(block, sides, width):
    for axis, dim in sides:
        count = lax.axis_size(axis)
        forward = [(i, i + 1) for i in range(count - 1)]
        backward = [(target, source) for source, target in forward]
        low = lax.ppermute(
            lax.slice_in_dim(block, block.shape[dim] - width, None, axis=dim), axis, forward
        )
        high_part = lax.ppermute(lax.slice_in_dim(block, 0, width, axis=dim), axis, backward)
        block = jnp.concatenate([low, block, high_part], axis=dim)
    return block


def limited(left_diff, right_diff, selector):
    left_size = jnp.abs(left_diff)
    right_size = jnp.abs(right_diff)
    agreement = 0.5 * (jnp.sign(left_diff) + jnp.sign(right_diff))
    minmod_size = jnp.minimum(left_size, right_size)
    central_size = jnp.minimum(2.0 * minmod_size, 0.5 * jnp.abs(left_diff + right_diff))
    superbee_size = jnp.maximum(
        jnp.minimum(2.0 * left_size, right_size), jnp.minimum(left_size, 2.0 * right_size)
    )
    chosen = jnp.where(
        selector == 0.0, minmod_size, jnp.where(selector == 1.0, central_size, superbee_size)
    )
    return agreement * chosen


def advect(padded, selector, courant_col):
    differences = padded[:, 1:] - padded[:, :-1]
    slopes = limited(differences[:, :-1], differences[:, 1:], selector[:, 1:-1])
    centers = padded[:, 1:-1]
    forward = courant_col * (centers[:, :-1] + 0.5 * (1.0 - courant_col) * slopes[:, :-1])
    backward = courant_col * (centers[:, 1:] - 0.5 * (1.0 + courant_col) * slopes[:, 1:])
    fluxes = jnp.where(courant_col > 0.0, forward, backward)
    return padded[:, 2:-2] - (fluxes[:, 1:] - fluxes[:, :-1])


def advect_slab(field, selector, courant_part):
    stacked = jnp.stack([field, selector.astype(jnp.float32)])
    padded = padded_2(stacked, (("space", 2),), 2)
    return advect(padded[0], padded[1], courant_part[:, None])


def row_of(vector, blocks, width):
    n = vector.shape[0] // blocks
    return jnp.pad(vector.reshape(blocks, 1, n), ((0, 0), (0, 0), (0, width - n)))


def on_device(occupation, propagator, flags_first, flags_second, courant, weights):
    n_core = lax.axis_size("core")
    n_x = lax.axis_size("x")
    n_zh = lax.axis_size("zh")
    row_count = lax.axis_size("y") * n_core
    col_count = n_zh * n_x
    row_index = lax.axis_index("y") * n_core + lax.axis_index("core")
    col_index = lax.axis_index("zh") * n_x + lax.axis_index("x")
    local_modes, cells = occupation.shape
    tile = propagator.shape[0]
    weight_total = jnp.sum(weights)

    offset_first = (col_index * row_count + row_index) * local_modes
    weight_first = lax.dynamic_slice_in_dim(weights, offset_first, local_modes)
    courant_first = lax.dynamic_slice_in_dim(courant, offset_first, local_modes)
    shifted = advect_slab(occupation, flags_first, courant_first)
    gathered = lax.all_gather(shifted, ROWS, axis=0, tiled=True)
    weight_colblk = lax.dynamic_slice_in_dim(weights, col_index * tile, tile)
    heat_part = jnp.dot(weight_colblk, gathered, precision=highest)
    pw_part = jnp.dot(propagator, weight_colblk, precision=highest)
    product = jnp.dot(
        propagator, gathered, precision=high, preferred_element_type=jnp.float32
    ).reshape(col_count, local_modes, cells)
    extra = 8 - 2
    payload = jnp.concatenate(
        [
            product,
            jnp.broadcast_to(heat_part[None, None, :], (col_count, 1, cells)),
            row_of(pw_part, col_count, cells),
            jnp.zeros((col_count, extra, cells), jnp.float32),
        ],
        axis=1,
    )
    depth = payload.shape[1]
    payload = payload.reshape(n_zh, n_x, depth, cells).transpose(1, 0, 2, 3)
    payload = payload.reshape(n_x * n_zh * depth, cells)
    payload = lax.psum_scatter(payload, "x", scatter_dimension=0, tiled=True)
    summed = lax.psum_scatter(payload, "zh", scatter_dimension=0, tiled=True)
    heat = summed[local_modes] / weight_total
    pw_second = summed[local_modes + 1, :local_modes]
    offset_second = (row_index * col_count + col_index) * local_modes
    weight_second = lax.dynamic_slice_in_dim(weights, offset_second, local_modes)
    courant_second = lax.dynamic_slice_in_dim(courant, offset_second, local_modes)
    middle = summed[:local_modes] + (weight_second - pw_second)[:, None] * heat[None, :]

    shifted_second = advect_slab(middle, flags_second, courant_second)
    gathered_second = lax.all_gather(shifted_second, "zh", axis=0, tiled=False)
    gathered_second = lax.all_gather(gathered_second, "x", axis=0, tiled=False)
    gathered_second = gathered_second.transpose(1, 0, 2, 3).reshape(tile, cells)
    weight_rowblk = lax.dynamic_slice_in_dim(weights, row_index * tile, tile)
    heat_part_second = jnp.dot(weight_rowblk, gathered_second, precision=highest)
    pw_part_second = jnp.dot(weight_rowblk, propagator, precision=highest)
    product_second = lax.dot_general(
        propagator,
        gathered_second,
        (((0,), (0,)), ((), ())),
        precision=high,
        preferred_element_type=jnp.float32,
    ).reshape(row_count, local_modes, cells)
    slots = jnp.where(
        jnp.arange(row_count)[:, None] == row_index, heat_part_second[None, :], 0.0
    )
    extra_second = 16 - row_count - 1
    payload_second = jnp.concatenate(
        [
            product_second,
            jnp.broadcast_to(slots[None], (row_count, row_count, cells)),
            row_of(pw_part_second, row_count, cells),
            jnp.zeros((row_count, extra_second, cells), jnp.float32),
        ],
        axis=1,
    )
    final_sum = lax.psum_scatter(payload_second, ROWS, scatter_dimension=0, tiled=True)[0]
    heat_slots = final_sum[local_modes : local_modes + row_count]
    heat_second = heat_slots[0]
    for k in range(1, row_count):
        heat_second = heat_second + heat_slots[k]
    heat_second = heat_second / weight_total
    pw_first = final_sum[local_modes + row_count, :local_modes]
    final = final_sum[:local_modes] + (weight_first - pw_first)[:, None] * heat_second[None, :]
    return (final, heat_second)


def solution(mesh):
    n_space, n_rows, n_cols = (mesh.shape[a] for a in ("space", "rows", "cols"))
    split = Mesh(
        mesh.devices.reshape(n_space, n_rows // 2, 2, 2, n_cols // 2),
        ("space", "y", "core", "zh", "x"),
    )
    mode_cr = ("zh", "x", "y", "core")
    mode_rc = ("y", "core", "zh", "x")
    placed = (
        P(mode_cr, "space"),
        P(ROWS, COLS),
        P(mode_cr, "space"),
        P(mode_rc, "space"),
        P(),
        P(),
    )
    return jax.shard_map(
        on_device,
        mesh=split,
        in_specs=placed,
        out_specs=(P(mode_cr, "space"), P("space")),
        check_vma=False,
    )
```

time: 768 us -> 315 us (0.41)
  blocking collectives: 404 us -> 13 us
  waiting for transfers between devices: 266 us -> 191 us
    psum x2 -> x0, blocking collectives: 404 us -> none  [heat_all(): lax.psum(jnp.dot(weight_part, shifted, precision=highest), ('rows', 'cols'))]
    all_gather x2, waiting for transfers between devices: 116 us -> 65 us  [the longest x1 41.5 us: on_device(): gathered_second = lax.all_gather(gathered_second, 'x', axis=0, tiled=False)]
    reduce_scatter x2 -> x3, waiting for transfers between devices: 140 us -> 120 us  [the longest x1 40.7 us: on_device(): payload = lax.psum_scatter(payload, 'x', scatter_dimension=0, tiled=True)]
    all_gather x0 -> x1, blocking collectives: none -> 13 us  [on_device(): gathered_second = lax.all_gather(shifted_second, 'zh', axis=0, tiled=False)]
    dot_general x4 -> x6, matrix products: 53.3 us -> 54.7 us  [the longest x1 19.7 us: on_device(): jnp.dot(propagator, gathered, precision=high, preferred_element_type=jnp....]
  transfers between devices with their start and end apart: 8 -> 9, of which waited for: 7 -> 9; matrix products, arithmetic and copies ran while one was open for 0% -> 6% of each run, Pallas kernels for 0% -> 0%
where the time goes in v1:
time: 315 us
  waiting for transfers between devices  191 us (61%)
  matrix products  54.7 us (17%)
  other arithmetic  18.5 us (6%)
  between operations  14 us (4%)
  blocking collectives  13 us (4%)
  starting transfers between devices  12.1 us (4%)
  local copies, waits for them, and re-layouts  11.2 us (4%)
    all_gather x1, waiting for transfers between devices, on_device(): gathered_second = lax.all_gather(gathered_second, 'x', axis=0, tiled=False)  41.5 us
    reduce_scatter x1, waiting for transfers between devices, on_device(): payload = lax.psum_scatter(payload, 'x', scatter_dimension=0, tiled=True)  40.7 us
    reduce_scatter x1, waiting for transfers between devices, on_device(): lax.psum_scatter(payload_second, ROWS, scatter_dimension=0, tiled=True)[0]  40.1 us
    reduce_scatter x1, waiting for transfers between devices, on_device(): summed = lax.psum_scatter(payload, 'zh', scatter_dimension=0, tiled=True)  38.9 us
    all_gather x1, waiting for transfers between devices, on_device(): gathered = lax.all_gather(shifted, ROWS, axis=0, tiled=True)  23.5 us
    dot_general x1, matrix products, on_device(): jnp.dot(propagator, gathered, precision=high, preferred_element_type=jnp....  19.7 us
    all_gather x1, blocking collectives, on_device(): gathered_second = lax.all_gather(shifted_second, 'zh', axis=0, tiled=False)  13 us
    dot_general x1, matrix products, on_device(): lax.dot_general(propagator, gathered_second, (((0,), (0,)), ((), ())), pr...  12.7 us
  transfers between devices with their start and end apart: 9, of which 9 were waited for; matrix products, arithmetic and copies ran while one was open for 6% of the time, Pallas kernels for 0%

profile of v1, /device:TPU:2, one launch (start us, length us, event | category | flops | bytes accessed | tf_op | source)
XLA Modules:
  0.0 314.6 jit_solution(16314916584973017809)
XLA Ops:
  7.2 0.0 all-gather.5.cloned.1.call-start
  7.2 1.0 convert_bitcast_fusion.1
  8.2 1.1 pad_maximum_fusion.5
  9.3 1.3 collective-permute-start.1
  10.6 4.6 %collective-permute-start = (f32[2,192,2]{2,1,0:T(8,128)S(1)}, f32[2,192,2]{2,1,0:T(8,128)S(1)}, u32[]{:S(2)}, u32[]{:S(2)}) collective-permute-start(f32[2,192,2]{2,1,0:T(8,128)S(1)} %get-tuple-element.12), channel_id=1, source_target_pairs={{0,64},{64,128},{128,192},{1,65},{65,129},{129,193},{2,66},{66,130... | collective-permute-start | bytes 9224 | tf_op jit(solution)/shard_map/ppermute | solution.py:19
  15.2 0.9 broadcast_compare_fusion
  16.0 2.0 collective-permute-done.1
  18.0 1.2 collective-permute-done
  19.2 1.4 pad_maximum_fusion
  20.6 0.1 slice_bitcast_fusion.2
  20.6 0.2 slice_subtract_fusion.1
  20.9 0.6 select_multiply_fusion.1
  21.5 0.6 fusion.9
  22.0 1.0 fusion.15
  23.1 0.0 all-gather.5.cloned.1.call-update
  23.1 0.2 reduce-scatter.4.cloned.1.call-start
  23.3 0.1 fusion.17
  23.4 10.2 %convolution_reduce_fusion.1 = f32[1536]{0:T(1024)S(1)} fusion(f32[1536,1]{0,1:T(1,128)S(1)} %reshape.156, f32[1536,1536]{1,0:T(8,128)} %param.7), kind=kOutput, calls=%fused_computation.9 | convolution fusion | flops 28311552 | bytes 9449472 | tf_op jit(solution)/shard_map/dot_general | solution.py:82
  33.6 0.1 reshape.144
  33.7 0.1 pad.22.clone
  33.8 23.5 %all-gather.5.cloned.1.call-done = f32[1536,512]{1,0:T(8,128)} async-done(((f32[192,512]{1,0:T(8,128)}), f32[1536,512]{1,0:T(8,128)}) %all-gather.5.cloned.1.call-update) | async-done | bytes 3145744 | tf_op jit(solution)/shard_map/all_gather | solution.py:79
  57.3 19.7 %convolution_bitcast_fusion.1 = f32[1536,512]{0,1:T(8,128)} fusion(f32[1536,512]{1,0:T(8,128)} %all-gather.5.cloned.1.call-done, f32[1536,1536]{1,0:T(8,128)} %param.7), kind=kOutput, calls=%fused_computation.7 | convolution fusion | flops 7247757312 | bytes 15728640 | tf_op jit(solution)/shard_map/dot_general | solution.py:83
  77.0 2.6 copy.16
  79.6 3.5 %fusion.18 = f32[1,512]{1,0:T(1,128)S(1)} fusion(f32[1536,1]{0,1:T(1,128)S(1)} %reshape.156, f32[1536,512]{1,0:T(8,128)} %all-gather.5.cloned.1.call-done), kind=kOutput, calls=%fused_computation.68 | convolution fusion | flops 9437184 | bytes 3153920 | tf_op jit(solution)/shard_map/dot_general | solution.py:81
  83.1 0.5 maximum_bitcast_fusion
  83.6 2.1 copy.17
  85.7 0.0 reduce-scatter.6.cloned.1.call-start
  85.7 40.7 %reduce-scatter.4.cloned.1.call-done = f32[400,512]{1,0:T(8,128)} async-done(((f32[1600,512]{1,0:T(8,128)}), f32[400,512]{1,0:T(8,128)}) %reduce-scatter.4.cloned.1.call-update) | async-done | bytes 819216 | tf_op jit(solution)/shard_map/reduce_scatter | solution.py:99
  126.4 0.0 all-gather.7.cloned.1.call-start
  126.5 0.6 reduce_sum.9
  127.1 38.9 %reduce-scatter.6.cloned.1.call-done = f32[200,512]{1,0:T(8,128)} async-done(((f32[400,512]{1,0:T(8,128)}), f32[200,512]{1,0:T(8,128)}) %reduce-scatter.6.cloned.1.call-update) | async-done | bytes 409616 | tf_op jit(solution)/shard_map/reduce_scatter | solution.py:100
  166.0 0.7 slice.223
  166.7 0.1 dynamic-slice_subtract_fusion.1
  166.8 1.4 slice_divide_fusion
  168.2 1.1 fusion.14
  169.3 0.1 pad_maximum_fusion.3
  169.4 1.3 collective-permute-start.3
  170.7 4.6 %collective-permute-start.2 = (f32[2,192,2]{2,1,0:T(8,128)S(1)}, f32[2,192,2]{2,1,0:T(8,128)S(1)}, u32[]{:S(2)}, u32[]{:S(2)}) collective-permute-start(f32[2,192,2]{2,1,0:T(8,128)S(1)} %get-tuple-element.10), channel_id=1, source_target_pairs={{0,64},{64,128},{128,192},{1,65},{65,129},{129,193},{2,66},{66,130... | collective-permute-start | bytes 9224 | tf_op jit(solution)/shard_map/ppermute | solution.py:19
  175.3 1.7 collective-permute-done.3
  177.0 1.5 collective-permute-done.2
  178.4 0.4 pad_maximum_fusion.1
  178.8 0.1 slice_bitcast_fusion
  178.9 0.2 slice_subtract_fusion
  179.1 0.6 select_multiply_fusion
  179.7 0.6 fusion.4
  180.3 0.3 fusion.13
  180.5 13.0 %all-gather = f32[384,512]{1,0:T(8,128)} all-gather(f32[192,512]{1,0:T(8,128)S(1)} %fusion.13), channel_id=2, replica_groups=mesh['space'=4,'y'=4,'core'=2,'zh'=2,'x'=4] {'zh'}, dimensions={0}, use_global_device_ids=true | all-gather | bytes 1179648 | tf_op jit(solution)/shard_map/all_gather | solution.py:109
  193.5 0.0 all-gather.7.cloned.1.call-update
  193.5 0.0 reduce-scatter.8.cloned.1.call-start
  193.6 7.0 %convolution_reduce_fusion = f32[1536]{0:T(1024)S(1)} fusion(f32[1536,1]{0,1:T(1,128)S(1)} %reshape.160, f32[1536,1536]{1,0:T(8,128)} %param.7), kind=kOutput, calls=%fused_computation.8 | convolution fusion | flops 28311552 | bytes 9449472 | tf_op jit(solution)/shard_map/dot_general | solution.py:114
  200.6 0.1 reshape.148
  200.7 0.1 pad.12.clone
  200.8 41.5 %all-gather.7.cloned.1.call-done = f32[8,192,512]{2,1,0:T(8,128)} async-done(((f32[2,192,512]{2,1,0:T(8,128)}), f32[8,192,512]{2,1,0:T(8,128)}) %all-gather.7.cloned.1.call-update) | async-done | bytes 3145744 | tf_op jit(solution)/shard_map/all_gather | solution.py:110
  242.3 2.2 copy.18
  244.5 1.6 fusion.19
  246.1 12.7 %convolution_bitcast_fusion = f32[1536,512]{0,1:T(8,128)} fusion(f32[1536,512]{1,0:T(8,128)S(1)} %bitcast.57, f32[1536,1536]{1,0:T(8,128)} %param.7), kind=kOutput, calls=%fused_computation.6 | convolution fusion | flops 7247757312 | bytes 15728640 | tf_op jit(solution)/shard_map/dot_general | solution.py:115
  258.8 2.4 copy.19
  261.2 0.1 broadcast_select_fusion
  261.3 2.3 fusion
  263.6 40.1 %reduce-scatter.8.cloned.1.call-done = f32[1,208,512]{2,1,0:T(8,128)} async-done(((f32[8,208,512]{2,1,0:T(8,128)}), f32[1,208,512]{2,1,0:T(8,128)}) %reduce-scatter.8.cloned.1.call-update) | async-done | bytes 426000 | tf_op jit(solution)/shard_map/reduce_scatter | solution.py:135
  303.7 0.7 slice.240
  304.4 0.1 dynamic-slice_subtract_fusion
  304.5 1.7 fusion.16
  306.2 1.8 fusion.12
  (21 shorter events, 0.2 us)
Async XLA Ops:
  7.2 50.1 %all-gather.5.cloned.1.call-start = ((), (), s32[]{:S(2)}) async-start(), calls=%async_computation.3 | async-start | bytes 3538944 | tf_op jit(solution)/shard_map/all_gather | solution.py:79
  9.3 8.7 %collective-permute-start.1 = (f32[2,192,2]{2,1,0:T(8,128)S(1)}, f32[2,192,2]{2,1,0:T(8,128)S(1)}, u32[]{:S(2)}, u32[]{:S(2)}) collective-permute-start(f32[2,192,2]{2,1,0:T(8,128)S(1)} %get-tuple-element.13), channel_id=1, source_target_pairs={{64,0},{128,64},{192,128},{65,1},{129,65},{193,129},{66,2},{130,66... | collective-permute-start | bytes 9224 | tf_op jit(solution)/shard_map/ppermute | solution.py:22
  10.6 8.6 %collective-permute-start = (f32[2,192,2]{2,1,0:T(8,128)S(1)}, f32[2,192,2]{2,1,0:T(8,128)S(1)}, u32[]{:S(2)}, u32[]{:S(2)}) collective-permute-start(f32[2,192,2]{2,1,0:T(8,128)S(1)} %get-tuple-element.12), channel_id=1, source_target_pairs={{0,64},{64,128},{128,192},{1,65},{65,129},{129,193},{2,66},{66,130... | collective-permute-start | bytes 9224 | tf_op jit(solution)/shard_map/ppermute | solution.py:19
  20.8 2.5 copy-start.1
  23.1 103.3 %reduce-scatter.4.cloned.1.call-start = ((), (), s32[]{:S(2)}) async-start(), calls=%async_computation.4 | async-start | bytes 4096000 | tf_op jit(solution)/shard_map/reduce_scatter | solution.py:99
  85.7 41.5 %copy-start = (s32[192,512]{1,0:T(8,128)S(1)}, s32[192,512]{1,0:T(8,128)}, u32[]{:S(2)}) copy-start(s32[192,512]{1,0:T(8,128)} %param.9) | copy-start | bytes 1179652
  85.7 80.3 %reduce-scatter.6.cloned.1.call-start = ((), (), s32[]{:S(2)}) async-start(), calls=%async_computation.5 | async-start | bytes 1228800 | tf_op jit(solution)/shard_map/reduce_scatter | solution.py:100
  126.4 115.8 %all-gather.7.cloned.1.call-start = ((), (), s32[]{:S(2)}) async-start(), calls=%async_computation.7 | async-start | bytes 3932160 | tf_op jit(solution)/shard_map/all_gather | solution.py:110
  169.4 7.6 %collective-permute-start.3 = (f32[2,192,2]{2,1,0:T(8,128)S(1)}, f32[2,192,2]{2,1,0:T(8,128)S(1)}, u32[]{:S(2)}, u32[]{:S(2)}) collective-permute-start(f32[2,192,2]{2,1,0:T(8,128)S(1)} %get-tuple-element.11), channel_id=1, source_target_pairs={{64,0},{128,64},{192,128},{65,1},{129,65},{193,129},{66,2},{130,66... | collective-permute-start | bytes 9224 | tf_op jit(solution)/shard_map/ppermute | solution.py:22
  170.7 7.7 %collective-permute-start.2 = (f32[2,192,2]{2,1,0:T(8,128)S(1)}, f32[2,192,2]{2,1,0:T(8,128)S(1)}, u32[]{:S(2)}, u32[]{:S(2)}) collective-permute-start(f32[2,192,2]{2,1,0:T(8,128)S(1)} %get-tuple-element.10), channel_id=1, source_target_pairs={{0,64},{64,128},{128,192},{1,65},{65,129},{129,193},{2,66},{66,130... | collective-permute-start | bytes 9224 | tf_op jit(solution)/shard_map/ppermute | solution.py:19
  193.5 110.2 %reduce-scatter.8.cloned.1.call-start = ((), (), s32[]{:S(2)}) async-start(), calls=%async_computation.6 | async-start | bytes 3833856 | tf_op jit(solution)/shard_map/reduce_scatter | solution.py:135
  306.2 1.9 copy-start.2
Sparse Core Ops, SparseCore 0:
  23.2 34.0 all-gather.4
  85.8 40.5 reduce-scatter.3
  128.9 37.0 reduce-scatter.5
  193.6 48.5 all-gather.6
  263.7 39.9 reduce-scatter.7

commit v2 on v1

--- a/solution.py
+++ b/solution.py
@@ -97,7 +97,12 @@
     payload = payload.reshape(n_zh, n_x, depth, cells).transpose(1, 0, 2, 3)
     payload = payload.reshape(n_x * n_zh * depth, cells)
     payload = lax.psum_scatter(payload, "x", scatter_dimension=0, tiled=True)
-    summed = lax.psum_scatter(payload, "zh", scatter_dimension=0, tiled=True)
+    payload = payload.reshape(n_zh, depth, cells)
+    zh_index = lax.axis_index("zh")
+    swap = [(0, 1), (1, 0)]
+    mine = lax.dynamic_index_in_dim(payload, zh_index, 0, keepdims=False)
+    theirs = lax.dynamic_index_in_dim(payload, 1 - zh_index, 0, keepdims=False)
+    summed = mine + lax.ppermute(theirs, "zh", swap)
     heat = summed[local_modes] / weight_total
     pw_second = summed[local_modes + 1, :local_modes]
     offset_second = (row_index * col_count + col_index) * local_modes
@@ -106,7 +111,12 @@
     middle = summed[:local_modes] + (weight_second - pw_second)[:, None] * heat[None, :]
 
     shifted_second = advect_slab(middle, flags_second, courant_second)
-    gathered_second = lax.all_gather(shifted_second, "zh", axis=0, tiled=False)
+    partner = lax.ppermute(shifted_second, "zh", swap)
+    gathered_second = jnp.where(
+        zh_index == 0,
+        jnp.stack([shifted_second, partner]),
+        jnp.stack([partner, shifted_second]),
+    )
     gathered_second = lax.all_gather(gathered_second, "x", axis=0, tiled=False)
     gathered_second = gathered_second.transpose(1, 0, 2, 3).reshape(tile, cells)
     weight_rowblk = lax.dynamic_slice_in_dim(weights, row_index * tile, tile)

time: 315 us -> 303 us (0.962)
  waiting for transfers between devices: 191 us -> 173 us
  starting transfers between devices: 12.1 us -> 29.4 us
  blocking collectives: 13 us -> 0 us
    reduce_scatter x1 -> x0, waiting for transfers between devices: 38.9 us -> none  [on_device(): summed = lax.psum_scatter(payload, 'zh', scatter_dimension=0, tiled=True)]
    ppermute x0 -> x2, waiting for transfers between devices: none -> 18.6 us  [the longest x1 12.5 us: on_device(): summed = mine + lax.ppermute(theirs, 'zh', swap)]
    ppermute x0 -> x2, starting transfers between devices: none -> 13.5 us  [the longest x1 7.7 us: on_device(): partner = lax.ppermute(shifted_second, 'zh', swap)]
    all_gather x1 -> x0, blocking collectives: 13 us -> none  [on_device(): gathered_second = lax.all_gather(shifted_second, 'zh', axis=0, tiled=False)]
    ppermute x2, starting transfers between devices: 9.12 us -> 12.9 us  [padded_2(): lax.ppermute(lax.slice_in_dim(block, block.shape[dim] - width, None, axis...]
  transfers between devices with their start and end apart: 9 -> 10, of which waited for: 9 -> 10; matrix products, arithmetic and copies ran while one was open for 6% -> 6% of each run, Pallas kernels for 0% -> 0%
where the time goes in v2:
time: 303 us; the launch traced here: 302 us
  waiting for transfers between devices  173 us (57%)
  matrix products  57.4 us (19%)
  starting transfers between devices  29.4 us (10%)
  other arithmetic  18.8 us (6%)
  between operations  14.1 us (5%)
  local copies, waits for them, and re-layouts  9.36 us (3%)
    all_gather x1, waiting for transfers between devices, on_device(): gathered_second = lax.all_gather(gathered_second, 'x', axis=0, tiled=False)  43.9 us
    reduce_scatter x1, waiting for transfers between devices, on_device(): payload = lax.psum_scatter(payload, 'x', scatter_dimension=0, tiled=True)  40.7 us
    reduce_scatter x1, waiting for transfers between devices, on_device(): lax.psum_scatter(payload_second, ROWS, scatter_dimension=0, tiled=True)[0]  40.1 us
    all_gather x1, waiting for transfers between devices, on_device(): gathered = lax.all_gather(shifted, ROWS, axis=0, tiled=True)  23.5 us
    dot_general x1, matrix products, on_device(): jnp.dot(propagator, gathered, precision=high, preferred_element_type=jnp....  19.6 us
    dot_general x1, matrix products, on_device(): lax.dot_general(propagator, gathered_second, (((0,), (0,)), ((), ())), pr...  13.4 us
    ppermute x2, starting transfers between devices, padded_2(): lax.ppermute(lax.slice_in_dim(block, block.shape[dim] - width, None, axis...  12.9 us
    ppermute x1, waiting for transfers between devices, on_device(): summed = mine + lax.ppermute(theirs, 'zh', swap)  12.5 us
  transfers between devices with their start and end apart: 10, of which 10 were waited for; matrix products, arithmetic and copies ran while one was open for 6% of the time, Pallas kernels for 0%

profile of v2, /device:TPU:2, one launch (start us, length us, event | category | flops | bytes accessed | tf_op | source)
XLA Modules:
  0.0 302.1 jit_solution(17435690708434316001)
XLA Ops:
  7.2 0.0 all-gather.3.cloned.1.call-start
  7.2 1.0 convert_bitcast_fusion.1
  8.2 1.1 pad_maximum_fusion.5
  9.3 1.3 collective-permute-start.1
  10.6 4.6 %collective-permute-start = (f32[2,192,2]{2,1,0:T(8,128)S(1)}, f32[2,192,2]{2,1,0:T(8,128)S(1)}, u32[]{:S(2)}, u32[]{:S(2)}) collective-permute-start(f32[2,192,2]{2,1,0:T(8,128)S(1)} %get-tuple-element.12), channel_id=1, source_target_pairs={{0,64},{64,128},{128,192},{1,65},{65,129},{129,193},{2,66},{66,130... | collective-permute-start | bytes 9224 | tf_op jit(solution)/shard_map/ppermute | solution.py:19
  15.2 0.9 broadcast_compare_fusion
  16.0 2.0 collective-permute-done.1
  18.0 1.2 collective-permute-done
  19.2 1.4 pad_maximum_fusion
  20.6 0.1 slice_bitcast_fusion.2
  20.6 0.2 slice_subtract_fusion.1
  20.9 0.6 select_multiply_fusion.1
  21.5 0.6 fusion.9
  22.0 1.0 fusion.15
  23.1 0.2 reduce-scatter.3.cloned.1.call-start
  23.3 0.1 fusion.17
  23.4 10.2 %convolution_reduce_fusion.1 = f32[1536]{0:T(1024)S(1)} fusion(f32[1536,1]{0,1:T(1,128)S(1)} %reshape.217, f32[1536,1536]{1,0:T(8,128)} %param.7), kind=kOutput, calls=%fused_computation.9 | convolution fusion | flops 28311552 | bytes 9449472 | tf_op jit(solution)/shard_map/dot_general | solution.py:82
  33.6 0.1 reshape.206
  33.7 0.1 pad.26.clone
  33.8 23.5 %all-gather.3.cloned.1.call-done = f32[1536,512]{1,0:T(8,128)} async-done(((f32[192,512]{1,0:T(8,128)}), f32[1536,512]{1,0:T(8,128)}) %all-gather.3.cloned.1.call-update) | async-done | bytes 3145744 | tf_op jit(solution)/shard_map/all_gather | solution.py:79
  57.3 19.6 %convolution_bitcast_fusion.1 = f32[1536,512]{0,1:T(8,128)} fusion(f32[1536,512]{1,0:T(8,128)} %all-gather.3.cloned.1.call-done, f32[1536,1536]{1,0:T(8,128)} %param.7), kind=kOutput, calls=%fused_computation.7 | convolution fusion | flops 7247757312 | bytes 15728640 | tf_op jit(solution)/shard_map/dot_general | solution.py:83
  76.9 2.6 copy.9
  79.5 3.5 %fusion.18 = f32[1,512]{1,0:T(1,128)S(1)} fusion(f32[1536,1]{0,1:T(1,128)S(1)} %reshape.217, f32[1536,512]{1,0:T(8,128)} %all-gather.3.cloned.1.call-done), kind=kOutput, calls=%fused_computation.71 | convolution fusion | flops 9437184 | bytes 3153920 | tf_op jit(solution)/shard_map/dot_general | solution.py:81
  83.0 0.5 maximum_bitcast_fusion
  83.5 2.0 copy.10
  85.6 0.0 all-gather.5.cloned.1.call-start
  85.6 40.7 %reduce-scatter.3.cloned.1.call-done = f32[400,512]{1,0:T(8,128)} async-done(((f32[1600,512]{1,0:T(8,128)}), f32[400,512]{1,0:T(8,128)}) %reduce-scatter.3.cloned.1.call-update) | async-done | bytes 819216 | tf_op jit(solution)/shard_map/reduce_scatter | solution.py:99
  126.3 1.0 dynamic-slice_bitcast_fusion
  127.4 5.8 %collective-permute-start.2 = (f32[200,512]{1,0:T(8,128)S(1)}, f32[200,512]{1,0:T(8,128)S(1)}, u32[]{:S(2)}, u32[]{:S(2)}) collective-permute-start(f32[200,512]{1,0:T(8,128)S(1)} %dynamic-slice_bitcast_fusion), channel_id=1, source_target_pairs={{0,4},{4,0},{1,5},{5,1},{2,6},{6,2},{3,7},{7,3},{8,12},{12,8},{9,1... | collective-permute-start | bytes 1228808 | tf_op jit(solution)/shard_map/ppermute | solution.py:105
  133.2 0.6 reduce_sum.9
  133.8 12.5 %collective-permute-done.2 = f32[200,512]{1,0:T(8,128)S(1)} collective-permute-done((f32[200,512]{1,0:T(8,128)S(1)}, f32[200,512]{1,0:T(8,128)S(1)}, u32[]{:S(2)}, u32[]{:S(2)}) %collective-permute-start.2) | collective-permute-done | bytes 409632 | tf_op jit(solution)/shard_map/ppermute | solution.py:105
  146.3 1.1 bitcast_add_fusion
  147.4 0.7 slice_divide_fusion
  148.1 0.1 dynamic-slice_subtract_fusion.1
  148.1 0.1 fusion.14
  148.3 0.1 pad_maximum_fusion.3
  148.4 1.3 collective-permute-start.4
  149.7 8.4 %collective-permute-start.3 = (f32[2,192,2]{2,1,0:T(8,128)S(1)}, f32[2,192,2]{2,1,0:T(8,128)S(1)}, u32[]{:S(2)}, u32[]{:S(2)}) collective-permute-start(f32[2,192,2]{2,1,0:T(8,128)S(1)} %get-tuple-element.10), channel_id=1, source_target_pairs={{0,64},{64,128},{128,192},{1,65},{65,129},{129,193},{2,66},{66,130... | collective-permute-start | bytes 9224 | tf_op jit(solution)/shard_map/ppermute | solution.py:19
  158.1 2.0 collective-permute-done.4
  160.0 1.2 collective-permute-done.3
  161.2 0.4 pad_maximum_fusion.1
  161.6 0.1 slice_bitcast_fusion
  161.7 0.2 slice_subtract_fusion
  161.9 0.6 select_multiply_fusion
  162.5 0.6 fusion.4
  163.1 0.3 fusion.13
  163.3 7.7 %collective-permute-start.5 = (f32[192,512]{1,0:T(8,128)S(1)}, f32[192,512]{1,0:T(8,128)S(1)}, u32[]{:S(2)}, u32[]{:S(2)}) collective-permute-start(f32[192,512]{1,0:T(8,128)S(1)} %fusion.13), channel_id=1, source_target_pairs={{0,4},{4,0},{1,5},{5,1},{2,6},{6,2},{3,7},{7,3},{8,12},{12,8},{9,1... | collective-permute-start | bytes 1179656 | tf_op jit(solution)/shard_map/ppermute | solution.py:114
  171.0 6.1 %collective-permute-done.5 = f32[192,512]{1,0:T(8,128)S(1)} collective-permute-done((f32[192,512]{1,0:T(8,128)S(1)}, f32[192,512]{1,0:T(8,128)S(1)}, u32[]{:S(2)}, u32[]{:S(2)}) %collective-permute-start.5) | collective-permute-done | bytes 393248 | tf_op jit(solution)/shard_map/ppermute | solution.py:114
  177.2 1.0 maximum_select_fusion
  178.2 0.0 reduce-scatter.5.cloned.1.call-start
  178.2 7.3 %convolution_reduce_fusion = f32[1536]{0:T(1024)S(1)} fusion(f32[1536,1]{0,1:T(1,128)S(1)} %reshape.221, f32[1536,1536]{1,0:T(8,128)} %param.7), kind=kOutput, calls=%fused_computation.8 | convolution fusion | flops 28311552 | bytes 9449472 | tf_op jit(solution)/shard_map/dot_general | solution.py:124
  185.5 0.1 reshape.211
  185.6 0.1 pad.12.clone
  185.7 43.9 %all-gather.5.cloned.1.call-done = f32[4,2,192,512]{3,2,0,1:T(8,128)} async-done(((f32[1,2,192,512]{3,2,0,1:T(8,128)}), f32[4,2,192,512]{3,2,0,1:T(8,128)}) %all-gather.5.cloned.1.call-update) | async-done | bytes 3145744 | tf_op jit(solution)/shard_map/all_gather | solution.py:120
  229.5 3.5 %fusion.19 = f32[1,512]{1,0:T(1,128)S(1)} fusion(f32[1536,1]{0,1:T(1,128)S(1)} %reshape.221, f32[1536,512]{1,0:T(8,128)} %bitcast.62), kind=kOutput, calls=%fused_computation.72 | convolution fusion | flops 9437184 | bytes 3153920 | tf_op jit(solution)/shard_map/dot_general | solution.py:123
  233.0 13.4 %convolution_bitcast_fusion = f32[1536,512]{0,1:T(8,128)} fusion(f32[1536,512]{1,0:T(8,128)} %bitcast.63, f32[1536,1536]{1,0:T(8,128)} %param.7), kind=kOutput, calls=%fused_computation.6 | convolution fusion | flops 7247757312 | bytes 15728640 | tf_op jit(solution)/shard_map/dot_general | solution.py:125
  246.4 2.4 copy.11
  248.7 0.1 broadcast_select_fusion
  248.8 2.3 fusion
  251.2 40.1 %reduce-scatter.5.cloned.1.call-done = f32[1,208,512]{2,1,0:T(8,128)} async-done(((f32[8,208,512]{2,1,0:T(8,128)}), f32[1,208,512]{2,1,0:T(8,128)}) %reduce-scatter.5.cloned.1.call-update) | async-done | bytes 426000 | tf_op jit(solution)/shard_map/reduce_scatter | solution.py:145
  291.3 0.7 slice.240
  292.0 0.1 dynamic-slice_subtract_fusion
  292.1 1.7 fusion.16
  293.8 1.8 fusion.12
  (23 shorter events, 0.2 us)
Async XLA Ops:
  7.2 50.1 %all-gather.3.cloned.1.call-start = ((), (), s32[]{:S(2)}) async-start(), calls=%async_computation.2 | async-start | bytes 3538944 | tf_op jit(solution)/shard_map/all_gather | solution.py:79
  9.3 8.7 %collective-permute-start.1 = (f32[2,192,2]{2,1,0:T(8,128)S(1)}, f32[2,192,2]{2,1,0:T(8,128)S(1)}, u32[]{:S(2)}, u32[]{:S(2)}) collective-permute-start(f32[2,192,2]{2,1,0:T(8,128)S(1)} %get-tuple-element.13), channel_id=1, source_target_pairs={{64,0},{128,64},{192,128},{65,1},{129,65},{193,129},{66,2},{130,66... | collective-permute-start | bytes 9224 | tf_op jit(solution)/shard_map/ppermute | solution.py:22
  10.6 8.6 %collective-permute-start = (f32[2,192,2]{2,1,0:T(8,128)S(1)}, f32[2,192,2]{2,1,0:T(8,128)S(1)}, u32[]{:S(2)}, u32[]{:S(2)}) collective-permute-start(f32[2,192,2]{2,1,0:T(8,128)S(1)} %get-tuple-element.12), channel_id=1, source_target_pairs={{0,64},{64,128},{128,192},{1,65},{65,129},{129,193},{2,66},{66,130... | collective-permute-start | bytes 9224 | tf_op jit(solution)/shard_map/ppermute | solution.py:19
  20.8 2.5 copy-start.1
  23.1 103.3 %reduce-scatter.3.cloned.1.call-start = ((), (), s32[]{:S(2)}) async-start(), calls=%async_computation.3 | async-start | bytes 4096000 | tf_op jit(solution)/shard_map/reduce_scatter | solution.py:99
  85.6 48.2 %copy-start = (s32[192,512]{1,0:T(8,128)S(1)}, s32[192,512]{1,0:T(8,128)}, u32[]{:S(2)}) copy-start(s32[192,512]{1,0:T(8,128)} %param.9) | copy-start | bytes 1179652
  85.6 143.9 %all-gather.5.cloned.1.call-start = ((), (), s32[]{:S(2)}) async-start(), calls=%async_computation.4 | async-start | bytes 3932160 | tf_op jit(solution)/shard_map/all_gather | solution.py:120
  127.4 19.0 %collective-permute-start.2 = (f32[200,512]{1,0:T(8,128)S(1)}, f32[200,512]{1,0:T(8,128)S(1)}, u32[]{:S(2)}, u32[]{:S(2)}) collective-permute-start(f32[200,512]{1,0:T(8,128)S(1)} %dynamic-slice_bitcast_fusion), channel_id=1, source_target_pairs={{0,4},{4,0},{1,5},{5,1},{2,6},{6,2},{3,7},{7,3},{8,12},{12,8},{9,1... | collective-permute-start | bytes 1228808 | tf_op jit(solution)/shard_map/ppermute | solution.py:105
  148.4 11.7 %collective-permute-start.4 = (f32[2,192,2]{2,1,0:T(8,128)S(1)}, f32[2,192,2]{2,1,0:T(8,128)S(1)}, u32[]{:S(2)}, u32[]{:S(2)}) collective-permute-start(f32[2,192,2]{2,1,0:T(8,128)S(1)} %get-tuple-element.11), channel_id=1, source_target_pairs={{64,0},{128,64},{192,128},{65,1},{129,65},{193,129},{66,2},{130,66... | collective-permute-start | bytes 9224 | tf_op jit(solution)/shard_map/ppermute | solution.py:22
  149.7 11.5 %collective-permute-start.3 = (f32[2,192,2]{2,1,0:T(8,128)S(1)}, f32[2,192,2]{2,1,0:T(8,128)S(1)}, u32[]{:S(2)}, u32[]{:S(2)}) collective-permute-start(f32[2,192,2]{2,1,0:T(8,128)S(1)} %get-tuple-element.10), channel_id=1, source_target_pairs={{0,64},{64,128},{128,192},{1,65},{65,129},{129,193},{2,66},{66,130... | collective-permute-start | bytes 9224 | tf_op jit(solution)/shard_map/ppermute | solution.py:19
  163.3 13.8 %collective-permute-start.5 = (f32[192,512]{1,0:T(8,128)S(1)}, f32[192,512]{1,0:T(8,128)S(1)}, u32[]{:S(2)}, u32[]{:S(2)}) collective-permute-start(f32[192,512]{1,0:T(8,128)S(1)} %fusion.13), channel_id=1, source_target_pairs={{0,4},{4,0},{1,5},{5,1},{2,6},{6,2},{3,7},{7,3},{8,12},{12,8},{9,1... | collective-permute-start | bytes 1179656 | tf_op jit(solution)/shard_map/ppermute | solution.py:114
  178.2 113.1 %reduce-scatter.5.cloned.1.call-start = ((), (), s32[]{:S(2)}) async-start(), calls=%async_computation.5 | async-start | bytes 3833856 | tf_op jit(solution)/shard_map/reduce_scatter | solution.py:145
  293.8 1.9 copy-start.2
Sparse Core Ops, SparseCore 0:
  23.2 34.0 all-gather.2
  85.7 40.5 reduce-scatter.2
  178.3 51.1 all-gather.4
  251.3 39.9 reduce-scatter.4

commit v3 on v1

--- a/solution.py
+++ b/solution.py
@@ -78,47 +78,74 @@
     shifted = advect_slab(occupation, flags_first, courant_first)
     gathered = lax.all_gather(shifted, ROWS, axis=0, tiled=True)
     weight_colblk = lax.dynamic_slice_in_dim(weights, col_index * tile, tile)
-    heat_part = jnp.dot(weight_colblk, gathered, precision=highest)
+    heat_part = jnp.sum(weight_colblk[:, None] * gathered, axis=0)
     pw_part = jnp.dot(propagator, weight_colblk, precision=highest)
-    product = jnp.dot(
-        propagator, gathered, precision=high, preferred_element_type=jnp.float32
-    ).reshape(col_count, local_modes, cells)
-    extra = 8 - 2
-    payload = jnp.concatenate(
-        [
-            product,
-            jnp.broadcast_to(heat_part[None, None, :], (col_count, 1, cells)),
-            row_of(pw_part, col_count, cells),
-            jnp.zeros((col_count, extra, cells), jnp.float32),
-        ],
-        axis=1,
-    )
-    depth = payload.shape[1]
-    payload = payload.reshape(n_zh, n_x, depth, cells).transpose(1, 0, 2, 3)
-    payload = payload.reshape(n_x * n_zh * depth, cells)
-    payload = lax.psum_scatter(payload, "x", scatter_dimension=0, tiled=True)
-    summed = lax.psum_scatter(payload, "zh", scatter_dimension=0, tiled=True)
-    heat = summed[local_modes] / weight_total
-    pw_second = summed[local_modes + 1, :local_modes]
+    chunks = 2
+    chunk = local_modes // chunks
+    blocks = propagator.reshape(col_count, chunks, chunk, tile)
     offset_second = (row_index * col_count + col_index) * local_modes
     weight_second = lax.dynamic_slice_in_dim(weights, offset_second, local_modes)
     courant_second = lax.dynamic_slice_in_dim(courant, offset_second, local_modes)
-    middle = summed[:local_modes] + (weight_second - pw_second)[:, None] * heat[None, :]
+    weight_rowblk = lax.dynamic_slice_in_dim(weights, row_index * tile, tile)
+    weight_rowparts = weight_rowblk.reshape(row_count, chunks, chunk)
+    zh_index = lax.axis_index("zh")
+    swap = [(0, 1), (1, 0)]
+    heat = None
+    pw_second = None
+    product_second = None
+    heat_part_second = None
+    for k in range(chunks):
+        rows_k = blocks[:, k].reshape(col_count * chunk, tile)
+        product = jnp.dot(
+            rows_k, gathered, precision=high, preferred_element_type=jnp.float32
+        ).reshape(col_count, chunk, cells)
+        parts = [product]
+        if k == 0:
+            parts += [
+                jnp.broadcast_to(heat_part[None, None, :], (col_count, 1, cells)),
+                row_of(pw_part, col_count, cells),
+                jnp.zeros((col_count, 6, cells), jnp.float32),
+            ]
+        payload = jnp.concatenate(parts, axis=1) if len(parts) > 1 else product
+        depth = payload.shape[1]
+        payload = payload.reshape(n_zh, n_x, depth, cells).transpose(1, 0, 2, 3)
+        payload = payload.reshape(n_x * n_zh * depth, cells)
+        payload = lax.psum_scatter(payload, "x", scatter_dimension=0, tiled=True)
+        payload = payload.reshape(n_zh, depth, cells)
+        mine = lax.dynamic_index_in_dim(payload, zh_index, 0, keepdims=False)
+        theirs = lax.dynamic_index_in_dim(payload, 1 - zh_index, 0, keepdims=False)
+        summed = mine + lax.ppermute(theirs, "zh", swap)
+        if k == 0:
+            heat = summed[chunk] / weight_total
+            pw_second = summed[chunk + 1, :local_modes]
+        part = slice(k * chunk, (k + 1) * chunk)
+        middle = summed[:chunk] + (weight_second[part] - pw_second[part])[:, None] * heat[None, :]
 
-    shifted_second = advect_slab(middle, flags_second, courant_second)
-    gathered_second = lax.all_gather(shifted_second, "zh", axis=0, tiled=False)
-    gathered_second = lax.all_gather(gathered_second, "x", axis=0, tiled=False)
-    gathered_second = gathered_second.transpose(1, 0, 2, 3).reshape(tile, cells)
-    weight_rowblk = lax.dynamic_slice_in_dim(weights, row_index * tile, tile)
-    heat_part_second = jnp.dot(weight_rowblk, gathered_second, precision=highest)
+        shifted_second = advect_slab(middle, flags_second[part], courant_second[part])
+        partner = lax.ppermute(shifted_second, "zh", swap)
+        pair = jnp.where(
+            zh_index == 0,
+            jnp.stack([shifted_second, partner]),
+            jnp.stack([partner, shifted_second]),
+        )
+        gathered_second = lax.all_gather(pair, "x", axis=0, tiled=False)
+        gathered_second = gathered_second.transpose(1, 0, 2, 3).reshape(col_count * chunk, cells)
+        weight_k = weight_rowparts[:, k].reshape(col_count * chunk)
+        heat_k = jnp.sum(weight_k[:, None] * gathered_second, axis=0)
+        product_k = lax.dot_general(
+            rows_k,
+            gathered_second,
+            (((0,), (0,)), ((), ())),
+            precision=high,
+            preferred_element_type=jnp.float32,
+        )
+        if k == 0:
+            heat_part_second, product_second = heat_k, product_k
+        else:
+            heat_part_second = heat_part_second + heat_k
+            product_second = product_second + product_k
     pw_part_second = jnp.dot(weight_rowblk, propagator, precision=highest)
-    product_second = lax.dot_general(
-        propagator,
-        gathered_second,
-        (((0,), (0,)), ((), ())),
-        precision=high,
-        preferred_element_type=jnp.float32,
-    ).reshape(row_count, local_modes, cells)
+    product_second = product_second.reshape(row_count, local_modes, cells)
     slots = jnp.where(
         jnp.arange(row_count)[:, None] == row_index, heat_part_second[None, :], 0.0
     )

time: 315 us -> 308 us (0.978); the launches traced: 315 us -> 303 us
  waiting for transfers between devices: 191 us -> 145 us
  starting transfers between devices: 12.1 us -> 37.8 us
  local copies, waits for them, and re-layouts: 11.2 us -> 25.8 us
  blocking collectives: 13 us -> 0 us
  other arithmetic: 18.5 us -> 23.9 us
    reduce_scatter x1 -> x0, waiting for transfers between devices: 38.9 us -> none  [on_device(): summed = lax.psum_scatter(payload, 'zh', scatter_dimension=0, tiled=True)]
    all_gather x1 -> x2, waiting for transfers between devices: 41.5 us -> 18.4 us  [on_device(): gathered_second = lax.all_gather(pair, 'x', axis=0, tiled=False)]
    ppermute x0 -> x4, waiting for transfers between devices: none -> 20.8 us  [the longest x2 16.1 us: on_device(): partner = lax.ppermute(shifted_second, 'zh', swap)]
    ppermute x0 -> x4, starting transfers between devices: none -> 19.5 us  [the longest x2 11.6 us: on_device(): summed = mine + lax.ppermute(theirs, 'zh', swap)]
    all_gather x1 -> x0, blocking collectives: 13 us -> none  [on_device(): gathered_second = lax.all_gather(shifted_second, 'zh', axis=0, tiled=False)]
    all_gather x1, waiting for transfers between devices: 23.5 us -> 12.8 us  [on_device(): gathered = lax.all_gather(shifted, ROWS, axis=0, tiled=True)]
    ppermute x2 -> x3, waiting for transfers between devices: 3.66 us -> 13.9 us  [padded_2(): lax.ppermute(lax.slice_in_dim(block, 0, width, axis=dim), axis, backward)]
    slice x1 -> x2, local copies, waits for them, and re-layouts: 0.7 us -> 8.81 us  [the longest x1 8.81 us: on_device(): rows_k = blocks[:, k].reshape(col_count * chunk, tile)]
  transfers between devices with their start and end apart: 9 -> 16, of which waited for: 9 -> 14; matrix products, arithmetic and copies ran while one was open for 6% -> 18% of each run, Pallas kernels for 0% -> 0%
where the time goes in v3:
time: 308 us; the launch traced here: 303 us
  waiting for transfers between devices  145 us (47%)
  matrix products  55.1 us (18%)
  starting transfers between devices  37.8 us (12%)
  local copies, waits for them, and re-layouts  25.8 us (8%)
  other arithmetic  23.9 us (8%)
  between operations  14.9 us (5%)
    reduce_scatter x1, waiting for transfers between devices, on_device(): lax.psum_scatter(payload_second, ROWS, scatter_dimension=0, tiled=True)[0]  40.1 us
    reduce_scatter x2, waiting for transfers between devices, on_device(): payload = lax.psum_scatter(payload, 'x', scatter_dimension=0, tiled=True)  35.5 us
    dot_general x2, matrix products, on_device(): jnp.dot(rows_k, gathered, precision=high, preferred_element_type=jnp.floa...  23 us
    all_gather x2, waiting for transfers between devices, on_device(): gathered_second = lax.all_gather(pair, 'x', axis=0, tiled=False)  18.4 us
    ppermute x2, waiting for transfers between devices, on_device(): partner = lax.ppermute(shifted_second, 'zh', swap)  16.1 us
    dot_general x2, matrix products, on_device(): lax.dot_general(rows_k, gathered_second, (((0,), (0,)), ((), ())), precis...  14.8 us
    ppermute x3, waiting for transfers between devices, padded_2(): lax.ppermute(lax.slice_in_dim(block, 0, width, axis=dim), axis, backward)  13.9 us
    ppermute x3, starting transfers between devices, padded_2(): lax.ppermute(lax.slice_in_dim(block, block.shape[dim] - width, None, axis...  13.8 us
  transfers between devices with their start and end apart: 16, of which 14 were waited for; matrix products, arithmetic and copies ran while one was open for 18% of the time, Pallas kernels for 0%

profile of v3, /device:TPU:2, one launch (start us, length us, event | category | flops | bytes accessed | tf_op | source)
XLA Modules:
  0.0 302.7 jit_solution(5444877252895187673)
XLA Ops:
  7.2 1.0 convert_bitcast_fusion
  8.2 1.1 pad_maximum_fusion.4
  9.3 3.8 %collective-permute-start = (f32[2,192,2]{2,1,0:T(8,128)S(1)}, f32[2,192,2]{2,1,0:T(8,128)S(1)}, u32[]{:S(2)}, u32[]{:S(2)}) collective-permute-start(f32[2,192,2]{2,1,0:T(8,128)S(1)} %get-tuple-element.8), channel_id=1, source_target_pairs={{0,64},{64,128},{128,192},{1,65},{65,129},{129,193},{2,66},{66,130... | collective-permute-start | bytes 9224 | tf_op jit(solution)/shard_map/ppermute | solution.py:19
  13.1 1.3 collective-permute-start.1
  14.5 0.8 broadcast_compare_fusion
  15.2 2.0 collective-permute-done
  17.3 4.3 %collective-permute-done.1 = f32[2,192,2]{2,1,0:T(8,128)S(1)} collective-permute-done((f32[2,192,2]{2,1,0:T(8,128)S(1)}, f32[2,192,2]{2,1,0:T(8,128)S(1)}, u32[]{:S(2)}, u32[]{:S(2)}) %collective-permute-start.1) | collective-permute-done | bytes 3104 | tf_op jit(solution)/shard_map/ppermute | solution.py:22
  21.6 1.4 pad_maximum_fusion
  23.2 0.6 select_multiply_fusion
  23.8 0.6 fusion.7
  24.4 1.0 fusion.11
  25.6 10.3 %convolution_reduce_fusion.1 = f32[1536]{0:T(1024)S(1)} fusion(f32[1536,1]{0,1:T(1,128)S(1)} %reshape.325, f32[1536,1536]{1,0:T(8,128)} %param.7), kind=kOutput, calls=%fused_computation.16 | convolution fusion | flops 28311552 | bytes 9449472 | tf_op jit(solution)/shard_map/dot_general | solution.py:82
  36.2 8.8 %fusion.30 = (f32[8,1,96,1536]{3,2,1,0:T(8,128)}, f32[8,1,96,1536]{3,2,1,0:T(8,128)}) fusion(f32[8,2,96,1536]{3,2,1,0:T(8,128)} %bitcast.105), kind=kLoop, calls=%fused_computation.105 | loop fusion | bytes 18874368 | tf_op jit(solution)/shard_map/slice | solution.py:98
  45.0 12.8 %all-gather.4.cloned.1.call-done = f32[1536,512]{1,0:T(8,128)} async-done(((f32[192,512]{1,0:T(8,128)}), f32[1536,512]{1,0:T(8,128)}) %all-gather.4.cloned.1.call-update) | async-done | bytes 3145744 | tf_op jit(solution)/shard_map/all_gather | solution.py:79
  57.8 12.0 %convolution_bitcast_fusion.1 = f32[768,512]{0,1:T(8,128)} fusion(f32[1536,512]{1,0:T(8,128)} %all-gather.4.cloned.1.call-done, f32[768,1536]{1,0:T(8,128)} %bitcast.108), kind=kOutput, calls=%fused_computation.14 | convolution fusion | flops 3623878656 | bytes 9437184 | tf_op jit(solution)/shard_map/dot_general | solution.py:99
  69.7 3.2 %copy.25 = f32[768,512]{1,0:T(8,128)} copy(f32[768,512]{0,1:T(8,128)} %convolution_bitcast_fusion.1) | data formatting | bytes 3145728 | tf_op jit(solution)/shard_map/dot_general | solution.py:99
  73.2 1.1 copy-done.1
  74.6 1.4 copy.26
  76.3 11.0 %convolution_bitcast_fusion = f32[768,512]{0,1:T(8,128)} fusion(f32[1536,512]{1,0:T(8,128)S(1)} %copy-done, f32[768,1536]{1,0:T(8,128)} %bitcast.106), kind=kOutput, calls=%fused_computation.13 | convolution fusion | flops 3623878656 | bytes 9437184 | tf_op jit(solution)/shard_map/dot_general | solution.py:99
  87.3 1.9 copy.28
  89.3 1.4 copy.29
  90.7 0.8 dynamic_slice.37
  91.5 12.4 %reduce-scatter.4.cloned.1.call-done = f32[208,512]{1,0:T(8,128)} async-done(((f32[832,512]{1,0:T(8,128)}), f32[208,512]{1,0:T(8,128)}) %reduce-scatter.4.cloned.1.call-update) | async-done | bytes 426000 | tf_op jit(solution)/shard_map/reduce_scatter | solution.py:113
  104.0 0.9 dynamic-slice_bitcast_fusion
  104.9 5.8 %collective-permute-start.2 = (f32[104,512]{1,0:T(8,128)S(1)}, f32[104,512]{1,0:T(8,128)S(1)}, u32[]{:S(2)}, u32[]{:S(2)}) collective-permute-start(f32[104,512]{1,0:T(8,128)S(1)} %dynamic-slice_bitcast_fusion), channel_id=1, source_target_pairs={{0,4},{4,0},{1,5},{5,1},{2,6},{6,2},{3,7},{7,3},{8,12},{12,8},{9,1... | collective-permute-start | bytes 638984 | tf_op jit(solution)/shard_map/ppermute | solution.py:117
  110.8 0.6 reduce_sum.37
  111.4 23.1 %reduce-scatter.6.cloned.1.call-done = f32[192,512]{1,0:T(8,128)} async-done(((f32[768,512]{1,0:T(8,128)}), f32[192,512]{1,0:T(8,128)}) %reduce-scatter.6.cloned.1.call-update) | async-done | bytes 393232 | tf_op jit(solution)/shard_map/reduce_scatter | solution.py:113
  134.5 0.9 dynamic-slice_bitcast_fusion.1
  135.5 5.8 %collective-permute-start.6 = (f32[96,512]{1,0:T(8,128)S(1)}, f32[96,512]{1,0:T(8,128)S(1)}, u32[]{:S(2)}, u32[]{:S(2)}) collective-permute-start(f32[96,512]{1,0:T(8,128)S(1)} %dynamic-slice_bitcast_fusion.1), channel_id=1, source_target_pairs={{0,4},{4,0},{1,5},{5,1},{2,6},{6,2},{3,7},{7,3},{8,12},{12,8},{9,1... | collective-permute-start | bytes 589832 | tf_op jit(solution)/shard_map/ppermute | solution.py:117
  141.3 1.0 bitcast_add_fusion
  142.3 0.7 slice_divide_fusion
  143.0 4.7 %collective-permute-done.6 = f32[96,512]{1,0:T(8,128)S(1)} collective-permute-done((f32[96,512]{1,0:T(8,128)S(1)}, f32[96,512]{1,0:T(8,128)S(1)}, u32[]{:S(2)}, u32[]{:S(2)}) %collective-permute-start.6) | collective-permute-done | bytes 196640 | tf_op jit(solution)/shard_map/ppermute | solution.py:117
  147.7 1.0 fusion.26
  148.8 4.3 %collective-permute-start.3 = (f32[2,96,2]{2,1,0:T(8,128)S(1)}, f32[2,96,2]{2,1,0:T(8,128)S(1)}, u32[]{:S(2)}, u32[]{:S(2)}) collective-permute-start(f32[2,96,2]{2,1,0:T(8,128)S(1)} %get-tuple-element.18), channel_id=1, source_target_pairs={{0,64},{64,128},{128,192},{1,65},{65,129},{129,193},{2,66},{66,130... | collective-permute-start | bytes 4616 | tf_op jit(solution)/shard_map/ppermute | solution.py:19
  153.2 1.3 collective-permute-start.4
  154.5 0.8 collective-permute-done.3
  155.4 5.3 %collective-permute-done.4 = f32[2,96,2]{2,1,0:T(8,128)S(1)} collective-permute-done((f32[2,96,2]{2,1,0:T(8,128)S(1)}, f32[2,96,2]{2,1,0:T(8,128)S(1)}, u32[]{:S(2)}, u32[]{:S(2)}) %collective-permute-start.4) | collective-permute-done | bytes 1568 | tf_op jit(solution)/shard_map/ppermute | solution.py:22
  161.0 0.3 select_multiply_fusion.2
  161.4 0.3 fusion.19
  161.9 4.3 %collective-permute-start.5 = (f32[96,512]{1,0:T(8,128)S(1)}, f32[96,512]{1,0:T(8,128)S(1)}, u32[]{:S(2)}, u32[]{:S(2)}) collective-permute-start(f32[96,512]{1,0:T(8,128)S(1)} %fusion.23), channel_id=1, source_target_pairs={{0,4},{4,0},{1,5},{5,1},{2,6},{6,2},{3,7},{7,3},{8,12},{12,8},{9,1... | collective-permute-start | bytes 589832 | tf_op jit(solution)/shard_map/ppermute | solution.py:125
  166.1 6.6 %collective-permute-done.5 = f32[96,512]{1,0:T(8,128)S(1)} collective-permute-done((f32[96,512]{1,0:T(8,128)S(1)}, f32[96,512]{1,0:T(8,128)S(1)}, u32[]{:S(2)}, u32[]{:S(2)}) %collective-permute-start.5) | collective-permute-done | bytes 196640 | tf_op jit(solution)/shard_map/ppermute | solution.py:125
  172.7 0.8 maximum_select_fusion
  173.7 5.6 %collective-permute-start.7 = (f32[2,96,2]{2,1,0:T(8,128)S(1)}, f32[2,96,2]{2,1,0:T(8,128)S(1)}, u32[]{:S(2)}, u32[]{:S(2)}) collective-permute-start(f32[2,96,2]{2,1,0:T(8,128)S(1)} %get-tuple-element.14), channel_id=1, source_target_pairs={{0,64},{64,128},{128,192},{1,65},{65,129},{129,193},{2,66},{66,130... | collective-permute-start | bytes 4616 | tf_op jit(solution)/shard_map/ppermute | solution.py:19
  179.3 1.5 collective-permute-start.8
  180.9 0.6 collective-permute-done.7
  181.5 4.3 %collective-permute-done.8 = f32[2,96,2]{2,1,0:T(8,128)S(1)} collective-permute-done((f32[2,96,2]{2,1,0:T(8,128)S(1)}, f32[2,96,2]{2,1,0:T(8,128)S(1)}, u32[]{:S(2)}, u32[]{:S(2)}) %collective-permute-start.8) | collective-permute-done | bytes 1568 | tf_op jit(solution)/shard_map/ppermute | solution.py:22
  186.2 0.3 select_multiply_fusion.1
  186.6 0.3 fusion.14
  187.1 3.6 %collective-permute-start.9 = (f32[96,512]{1,0:T(8,128)S(1)}, f32[96,512]{1,0:T(8,128)S(1)}, u32[]{:S(2)}, u32[]{:S(2)}) collective-permute-start(f32[96,512]{1,0:T(8,128)S(1)} %fusion.22), channel_id=1, source_target_pairs={{0,4},{4,0},{1,5},{5,1},{2,6},{6,2},{3,7},{7,3},{8,12},{12,8},{9,1... | collective-permute-start | bytes 589832 | tf_op jit(solution)/shard_map/ppermute | solution.py:125
  190.7 9.5 %collective-permute-done.9 = f32[96,512]{1,0:T(8,128)S(1)} collective-permute-done((f32[96,512]{1,0:T(8,128)S(1)}, f32[96,512]{1,0:T(8,128)S(1)}, u32[]{:S(2)}, u32[]{:S(2)}) %collective-permute-start.9) | collective-permute-done | bytes 196640 | tf_op jit(solution)/shard_map/ppermute | solution.py:125
  200.1 0.8 maximum_select_fusion.1
  201.1 7.0 %convolution_reduce_fusion = f32[1536]{0:T(1024)S(1)} fusion(f32[1536,1]{0,1:T(1,128)S(1)} %reshape.327, f32[1536,1536]{1,0:T(8,128)} %param.7), kind=kOutput, calls=%fused_computation.15 | convolution fusion | flops 28311552 | bytes 9449472 | tf_op jit(solution)/shard_map/dot_general | solution.py:147
  208.3 6.7 %fusion.34 = f32[512,1536]{1,0:T(8,128)S(1)} fusion(f32[768,512]{1,0:T(8,128)} %bitcast.112, f32[768,1536]{1,0:T(8,128)} %bitcast.109), kind=kOutput, calls=%fused_computation.109 | convolution fusion | flops 3623878656 | bytes 9437184 | tf_op jit(solution)/shard_map/dot_general | solution.py:135
  215.1 18.4 %all-gather.8.cloned.1.call-done = f32[4,2,96,512]{3,2,1,0:T(8,128)} async-done(((f32[1,2,96,512]{3,2,1,0:T(8,128)}), f32[4,2,96,512]{3,2,1,0:T(8,128)}) %all-gather.8.cloned.1.call-update) | async-done | bytes 1572880 | tf_op jit(solution)/shard_map/all_gather | solution.py:131
  233.5 1.5 copy.30
  235.0 8.0 %fusion.2 = f32[1536,512]{0,1:T(8,128)} fusion(f32[512,1536]{1,0:T(8,128)S(1)} %fusion.34, f32[768,512]{1,0:T(8,128)S(1)} %bitcast.114, f32[768,1536]{1,0:T(8,128)} %bitcast.107), kind=kOutput, calls=%fused_computation.6 | convolution fusion | flops 3624665088 | bytes 12582912 | tf_op jit(solution)/shard_map/dot_general | solution.py:135
  243.0 2.4 copy.31
  245.4 1.6 fusion.3
  247.0 1.6 fusion.4
  248.7 2.3 fusion
  251.0 40.1 %reduce-scatter.8.cloned.1.call-done = f32[1,208,512]{2,1,0:T(8,128)} async-done(((f32[8,208,512]{2,1,0:T(8,128)}), f32[1,208,512]{2,1,0:T(8,128)}) %reduce-scatter.8.cloned.1.call-update) | async-done | bytes 426000 | tf_op jit(solution)/shard_map/reduce_scatter | solution.py:162
  291.2 0.7 slice.381
  291.9 1.7 fusion.27
  293.6 1.8 fusion.10
  (62 shorter events, 3.7 us)
Async XLA Ops:
  7.2 50.6 %all-gather.4.cloned.1.call-start = ((), (), s32[]{:S(2)}) async-start(), calls=%async_computation.3 | async-start | bytes 3538944 | tf_op jit(solution)/shard_map/all_gather | solution.py:79
  9.3 8.0 %collective-permute-start = (f32[2,192,2]{2,1,0:T(8,128)S(1)}, f32[2,192,2]{2,1,0:T(8,128)S(1)}, u32[]{:S(2)}, u32[]{:S(2)}) collective-permute-start(f32[2,192,2]{2,1,0:T(8,128)S(1)} %get-tuple-element.8), channel_id=1, source_target_pairs={{0,64},{64,128},{128,192},{1,65},{65,129},{129,193},{2,66},{66,130... | collective-permute-start | bytes 9224 | tf_op jit(solution)/shard_map/ppermute | solution.py:19
  13.1 8.4 %collective-permute-start.1 = (f32[2,192,2]{2,1,0:T(8,128)S(1)}, f32[2,192,2]{2,1,0:T(8,128)S(1)}, u32[]{:S(2)}, u32[]{:S(2)}) collective-permute-start(f32[2,192,2]{2,1,0:T(8,128)S(1)} %get-tuple-element.9), channel_id=1, source_target_pairs={{64,0},{128,64},{192,128},{65,1},{129,65},{193,129},{66,2},{130,66... | collective-permute-start | bytes 9224 | tf_op jit(solution)/shard_map/ppermute | solution.py:22
  23.2 2.3 copy-start.3
  25.5 78.5 %reduce-scatter.4.cloned.1.call-start = ((), (), s32[]{:S(2)}) async-start(), calls=%async_computation.4 | async-start | bytes 2129920 | tf_op jit(solution)/shard_map/reduce_scatter | solution.py:113
  69.7 3.2 %copy-start = (f32[1536,512]{1,0:T(8,128)S(1)}, f32[1536,512]{1,0:T(8,128)}, u32[]{:S(2)}) copy-start(f32[1536,512]{1,0:T(8,128)} %all-gather.4.cloned.1.call-done) | copy-start | bytes 9437188
  72.9 1.4 copy-start.1
  76.0 58.5 %reduce-scatter.6.cloned.1.call-start = ((), (), s32[]{:S(2)}) async-start(), calls=%async_computation.6 | async-start | bytes 1966080 | tf_op jit(solution)/shard_map/reduce_scatter | solution.py:113
  89.2 2.3 copy-start.2
  90.7 117.7 %all-gather.6.cloned.1.call-start = ((), (), s32[]{:S(2)}) async-start(), calls=%async_computation.5 | async-start | bytes 1966080 | tf_op jit(solution)/shard_map/all_gather | solution.py:131
  104.9 36.4 %collective-permute-start.2 = (f32[104,512]{1,0:T(8,128)S(1)}, f32[104,512]{1,0:T(8,128)S(1)}, u32[]{:S(2)}, u32[]{:S(2)}) collective-permute-start(f32[104,512]{1,0:T(8,128)S(1)} %dynamic-slice_bitcast_fusion), channel_id=1, source_target_pairs={{0,4},{4,0},{1,5},{5,1},{2,6},{6,2},{3,7},{7,3},{8,12},{12,8},{9,1... | collective-permute-start | bytes 638984 | tf_op jit(solution)/shard_map/ppermute | solution.py:117
  135.5 12.2 %collective-permute-start.6 = (f32[96,512]{1,0:T(8,128)S(1)}, f32[96,512]{1,0:T(8,128)S(1)}, u32[]{:S(2)}, u32[]{:S(2)}) collective-permute-start(f32[96,512]{1,0:T(8,128)S(1)} %dynamic-slice_bitcast_fusion.1), channel_id=1, source_target_pairs={{0,4},{4,0},{1,5},{5,1},{2,6},{6,2},{3,7},{7,3},{8,12},{12,8},{9,1... | collective-permute-start | bytes 589832 | tf_op jit(solution)/shard_map/ppermute | solution.py:117
  148.8 6.5 %collective-permute-start.3 = (f32[2,96,2]{2,1,0:T(8,128)S(1)}, f32[2,96,2]{2,1,0:T(8,128)S(1)}, u32[]{:S(2)}, u32[]{:S(2)}) collective-permute-start(f32[2,96,2]{2,1,0:T(8,128)S(1)} %get-tuple-element.18), channel_id=1, source_target_pairs={{0,64},{64,128},{128,192},{1,65},{65,129},{129,193},{2,66},{66,130... | collective-permute-start | bytes 4616 | tf_op jit(solution)/shard_map/ppermute | solution.py:19
  153.2 7.5 %collective-permute-start.4 = (f32[2,96,2]{2,1,0:T(8,128)S(1)}, f32[2,96,2]{2,1,0:T(8,128)S(1)}, u32[]{:S(2)}, u32[]{:S(2)}) collective-permute-start(f32[2,96,2]{2,1,0:T(8,128)S(1)} %get-tuple-element.19), channel_id=1, source_target_pairs={{64,0},{128,64},{192,128},{65,1},{129,65},{193,129},{66,2},{130,66... | collective-permute-start | bytes 4616 | tf_op jit(solution)/shard_map/ppermute | solution.py:22
  161.9 10.9 %collective-permute-start.5 = (f32[96,512]{1,0:T(8,128)S(1)}, f32[96,512]{1,0:T(8,128)S(1)}, u32[]{:S(2)}, u32[]{:S(2)}) collective-permute-start(f32[96,512]{1,0:T(8,128)S(1)} %fusion.23), channel_id=1, source_target_pairs={{0,4},{4,0},{1,5},{5,1},{2,6},{6,2},{3,7},{7,3},{8,12},{12,8},{9,1... | collective-permute-start | bytes 589832 | tf_op jit(solution)/shard_map/ppermute | solution.py:125
  173.5 59.9 %all-gather.8.cloned.1.call-start = ((), (), s32[]{:S(2)}) async-start(), calls=%async_computation.7 | async-start | bytes 1966080 | tf_op jit(solution)/shard_map/all_gather | solution.py:131
  173.7 7.8 %collective-permute-start.7 = (f32[2,96,2]{2,1,0:T(8,128)S(1)}, f32[2,96,2]{2,1,0:T(8,128)S(1)}, u32[]{:S(2)}, u32[]{:S(2)}) collective-permute-start(f32[2,96,2]{2,1,0:T(8,128)S(1)} %get-tuple-element.14), channel_id=1, source_target_pairs={{0,64},{64,128},{128,192},{1,65},{65,129},{129,193},{2,66},{66,130... | collective-permute-start | bytes 4616 | tf_op jit(solution)/shard_map/ppermute | solution.py:19
  179.3 6.5 %collective-permute-start.8 = (f32[2,96,2]{2,1,0:T(8,128)S(1)}, f32[2,96,2]{2,1,0:T(8,128)S(1)}, u32[]{:S(2)}, u32[]{:S(2)}) collective-permute-start(f32[2,96,2]{2,1,0:T(8,128)S(1)} %get-tuple-element.15), channel_id=1, source_target_pairs={{64,0},{128,64},{192,128},{65,1},{129,65},{193,129},{66,2},{130,66... | collective-permute-start | bytes 4616 | tf_op jit(solution)/shard_map/ppermute | solution.py:22
  187.1 13.1 %collective-permute-start.9 = (f32[96,512]{1,0:T(8,128)S(1)}, f32[96,512]{1,0:T(8,128)S(1)}, u32[]{:S(2)}, u32[]{:S(2)}) collective-permute-start(f32[96,512]{1,0:T(8,128)S(1)} %fusion.22), channel_id=1, source_target_pairs={{0,4},{4,0},{1,5},{5,1},{2,6},{6,2},{3,7},{7,3},{8,12},{12,8},{9,1... | collective-permute-start | bytes 589832 | tf_op jit(solution)/shard_map/ppermute | solution.py:125
  201.0 90.2 %reduce-scatter.8.cloned.1.call-start = ((), (), s32[]{:S(2)}) async-start(), calls=%async_computation.8 | async-start | bytes 3833856 | tf_op jit(solution)/shard_map/reduce_scatter | solution.py:162
  293.6 1.9 copy-start.4
Sparse Core Ops, SparseCore 0:
  25.6 32.1 all-gather.3
  76.1 27.7 reduce-scatter.3
  106.5 27.9 reduce-scatter.5
  173.7 29.0 all-gather.5
  204.4 28.9 all-gather.7
  251.1 39.9 reduce-scatter.7
